TPU v7x, 512 devices: a whole 4x8x8 slice. The times are simulated.
512 devices in a mesh: dp: 32 (over y, z_hi), seq: 16 (over x, z_lo, core).
Axes of the slice: x: 4, y: 8, z: 8 (z_hi: 4, z_lo: 2; z = z_hi * 2 + z_lo), core: 2. Of those that a mesh axis runs over, the one named last changes fastest.
Arguments:
- queries: bfloat16 [32, 2048, 1024], P('dp', 'seq'), may hold values from -6 to 6
- key_input: bfloat16 [32, 2048, 1024], P('dp', 'seq'), may hold values from -6 to 6
- values: bfloat16 [32, 2048, 1024], P('dp', 'seq'), may hold values from -6 to 6
- cotangent: bfloat16 [32, 2048, 1024], P('dp', 'seq'), may hold values from -12 to 12
- tile_mask: int32 [32, 32, 32], P('dp'), may hold values from 0 to 1, as said below
- condition_flags: int32 [32, 2048], P('dp', 'seq'), may hold values 0 or 1
- condition_embed: float32 [2, 1024], replicated, may hold values from -4 to 4
Outputs:
- attended: bfloat16 [32, 2048, 1024], P('dp', 'seq')
- grad_queries: bfloat16 [32, 2048, 1024], P('dp', 'seq')
- grad_keys: bfloat16 [32, 2048, 1024], P('dp', 'seq')
- grad_values: bfloat16 [32, 2048, 1024], P('dp', 'seq')
- grad_condition: float32 [2, 1024], replicated
Inputs may be any that keep to these rules, and one draw needn't show every extreme that they name: tile_mask[b, i, i] is 1; tile_mask[b, i, j] is 0 unless j < 2 or the absolute difference of i // 2 and j // 2 is at most 1.
All inputs are finite; a program needn't handle non-finite values. No bound on the sum of `condition_flags` on one device may be relied on, other than what follows from the above.
Results may differ from a plain program's by a relative error of at most 0.008.
The roundings to bfloat16 on the way count: a program that leaves them out, or rounds other values in their place, can miss the bound.
Values may be sent and summed in bfloat16 or wider, within the bound.
No kernel may reach another device: no remote copies, remote signals or barrier semaphores. Data moves between devices by JAX's collectives and lax.ppermute only.
A program may use at most 64 MiB of HBM per device.

v0:
```python
import math
import jax
import jax.numpy as jnp
from jax import lax
from jax.sharding import PartitionSpec as P

HEAD_DIM = 128
BLOCK = 64
masked_score = -1e30


def contract_last(left, right):
    return lax.dot_general(
        left, right, (((1,), (1,)), ((), ())), preferred_element_type=jnp.float32
    )


def contract_first(left, right):
    return lax.dot_general(
        left, right, (((0,), (0,)), ((), ())), preferred_element_type=jnp.float32
    )


def attend_and_grads(query_eff, grad_rows, key_set, value_set, allowed, head_count, head_dim):
    score_scale = 1.0 / math.sqrt(head_dim)
    outputs = []
    log_list = []
    delta_list = []
    query_grads = []
    key_grads = []
    value_grads = []
    for head in range(head_count):
        first_col = head * head_dim
        last_col = first_col + head_dim
        scores = jnp.where(
            allowed,
            contract_last(query_eff[:, first_col:last_col], key_set[:, first_col:last_col])
            * score_scale,
            masked_score,
        )
        top = jnp.max(scores, axis=1, keepdims=True)
        total = jnp.sum(jnp.where(allowed, jnp.exp(scores - top), 0.0), axis=1, keepdims=True)
        log_total = top + jnp.log(total)
        weights = jnp.where(allowed, jnp.exp(scores - log_total), 0.0)
        weights_half = weights.astype(jnp.bfloat16)
        output = jnp.dot(
            weights_half, value_set[:, first_col:last_col], preferred_element_type=jnp.float32
        ).astype(jnp.bfloat16)
        head_grad = grad_rows[:, first_col:last_col]
        delta = jnp.sum(
            head_grad.astype(jnp.float32) * output.astype(jnp.float32), axis=1, keepdims=True
        )
        dprob = contract_last(head_grad, value_set[:, first_col:last_col])
        dscore = (weights * (dprob - delta) * score_scale).astype(jnp.bfloat16)
        query_grads.append(
            jnp.dot(dscore, key_set[:, first_col:last_col], preferred_element_type=jnp.float32)
        )
        key_grads.append(contract_first(dscore, query_eff[:, first_col:last_col]))
        value_grads.append(contract_first(weights_half, head_grad))
        outputs.append(output)
        log_list.append(log_total)
        delta_list.append(delta)
    return (
        jnp.concatenate(outputs, axis=1),
        jnp.concatenate(log_list, axis=1),
        jnp.concatenate(delta_list, axis=1),
        jnp.concatenate(query_grads, axis=1),
        jnp.concatenate(key_grads, axis=1),
        jnp.concatenate(value_grads, axis=1),
    )


def head_grads(
    query_eff, grad_rows, key_set, value_set, allowed, log_totals, deltas, head_count, head_dim
):
    score_scale = 1.0 / math.sqrt(head_dim)
    key_grads = []
    value_grads = []
    for head in range(head_count):
        first_col = head * head_dim
        last_col = first_col + head_dim
        scores = jnp.where(
            allowed,
            contract_last(query_eff[:, first_col:last_col], key_set[:, first_col:last_col])
            * score_scale,
            masked_score,
        )
        weights = jnp.where(allowed, jnp.exp(scores - log_totals[:, head : head + 1]), 0.0)
        dprob = contract_last(grad_rows[:, first_col:last_col], value_set[:, first_col:last_col])
        dscore = (weights * (dprob - deltas[:, head : head + 1]) * score_scale).astype(jnp.bfloat16)
        key_grads.append(contract_first(dscore, query_eff[:, first_col:last_col]))
        value_grads.append(
            contract_first(weights.astype(jnp.bfloat16), grad_rows[:, first_col:last_col])
        )
    return (jnp.concatenate(key_grads, axis=1), jnp.concatenate(value_grads, axis=1))


def expand_tiles(tiles, block_rows):
    return jnp.repeat(jnp.repeat(tiles, block_rows, axis=0), block_rows, axis=1) > 0


def body(queries, key_input, values, cotangent, tile_mask, condition_flags, condition_embed):
    graph_count = queries.shape[0] * lax.axis_size("dp")
    query_rows = queries[0]
    key_rows = key_input[0]
    value_rows = values[0]
    grad_rows = cotangent[0]
    tok_rows, width = query_rows.shape
    head_dim = HEAD_DIM
    head_count = width // head_dim
    block_rows = BLOCK
    query_blocks = tok_rows // block_rows
    seq_index = lax.axis_index("seq")
    seq_count = lax.axis_size("seq")
    flag_column = condition_flags[0].astype(jnp.float32)[:, None]
    query_eff = (query_rows.astype(jnp.float32) + flag_column * condition_embed[0][None, :]).astype(
        jnp.bfloat16
    )
    key_eff = (key_rows.astype(jnp.float32) + flag_column * condition_embed[1][None, :]).astype(
        jnp.bfloat16
    )
    tile_table = tile_mask[0]
    block_count = tile_table.shape[0]
    own_tiles = lax.dynamic_slice_in_dim(tile_table, seq_index * query_blocks, query_blocks, 0)
    slot_starts = [
        0,
        (seq_index - 1) * query_blocks,
        seq_index * query_blocks,
        (seq_index + 1) * query_blocks,
    ]
    slot_valid = [seq_index >= 2, seq_index >= 1, seq_index >= 0, seq_index <= seq_count - 2]
    slot_blocks = []
    slot_tiles = []
    for slot in range(4):
        start_block = jnp.clip(slot_starts[slot], 0, block_count - query_blocks)
        slot_blocks.append(start_block)
        columns = lax.dynamic_slice_in_dim(own_tiles, start_block, query_blocks, 1)
        slot_tiles.append(jnp.where(slot_valid[slot], columns, 0))
    allowed = expand_tiles(jnp.concatenate(slot_tiles, axis=1), block_rows)
    whole_keys, whole_values = (
        lax.all_gather(key_eff, "seq", axis=0, tiled=True),
        lax.all_gather(value_rows, "seq", axis=0, tiled=True),
    )
    key_set = jnp.concatenate(
        [
            lax.dynamic_slice_in_dim(whole_keys, slot_blocks[slot] * block_rows, tok_rows, 0)
            for slot in range(4)
        ],
        axis=0,
    )
    value_set = jnp.concatenate(
        [
            lax.dynamic_slice_in_dim(whole_values, slot_blocks[slot] * block_rows, tok_rows, 0)
            for slot in range(4)
        ],
        axis=0,
    )
    attended, log_totals, deltas, query_total, unused_keys, unused_values = attend_and_grads(
        query_eff, grad_rows, key_set, value_set, allowed, head_count, head_dim
    )
    partial_value = jnp.sum(flag_column * query_total, axis=0)
    all_logs, all_deltas = (
        lax.all_gather(log_totals, "seq", axis=0, tiled=True),
        lax.all_gather(deltas, "seq", axis=0, tiled=True),
    )
    own_columns = lax.dynamic_slice_in_dim(tile_table, seq_index * query_blocks, query_blocks, 1)
    allowed_columns = expand_tiles(own_columns, block_rows)
    query_piece = lax.all_gather(query_eff, "seq", axis=0, tiled=True)
    grad_piece = lax.all_gather(grad_rows, "seq", axis=0, tiled=True)
    grads = head_grads(
        query_piece,
        grad_piece,
        key_eff,
        value_rows,
        allowed_columns,
        all_logs,
        all_deltas,
        head_count,
        head_dim,
    )
    key_total = grads[0]
    value_total = grads[1]
    key_partial = jnp.sum(flag_column * key_total, axis=0)
    cond_grad = lax.psum(jnp.stack([partial_value, key_partial]), ("dp", "seq"))
    cond_grad = cond_grad / graph_count
    return (
        attended[None],
        query_total.astype(jnp.bfloat16)[None],
        key_total.astype(jnp.bfloat16)[None],
        value_total.astype(jnp.bfloat16)[None],
        cond_grad,
    )


def solution(mesh):
    placed = (
        P("dp", "seq", None),
        P("dp", "seq", None),
        P("dp", "seq", None),
        P("dp", "seq", None),
        P("dp", None, None),
        P("dp", "seq"),
        P(),
    )
    return jax.shard_map(
        body,
        mesh=mesh,
        in_specs=placed,
        out_specs=(
            P("dp", "seq", None),
            P("dp", "seq", None),
            P("dp", "seq", None),
            P("dp", "seq", None),
            P(),
        ),
        check_vma=False,
    )
```

profile of v0, /device:TPU:1, one launch (start us, length us, event | category | flops | bytes accessed | tf_op | source)
XLA Modules:
  0.0 366.1 jit_solution(12846601326392642082)
XLA Ops:
  14.2 1.8 copy.154
  19.6 50.2 %all-gather.7.cloned.1.call-done = bf16[2048,1024]{0,1:T(8,128)(2,1)} async-done(((bf16[128,1024]{0,1:T(8,128)(2,1)}), bf16[2048,1024]{0,1:T(8,128)(2,1)}) %all-gather.7.cloned.1.call-update) | async-done | bytes 4194320 | tf_op jit(solution)/shard_map/all_gather | solution.py:141
  69.8 1.9 fusion.386
  72.4 41.4 %all-gather.11.cloned.1.call-done = bf16[1,2048,1024]{2,1,0:T(8,128)(2,1)} async-done(((bf16[1,128,1024]{2,1,0:T(8,128)(2,1)}), bf16[1,2048,1024]{2,1,0:T(8,128)(2,1)}) %all-gather.11.cloned.1.call-update) | async-done | bytes 4194320 | tf_op jit(solution)/shard_map/all_gather | solution.py:142
  131.6 2.0 constant_dynamic-update-slice_fusion.15
  133.6 2.0 constant_dynamic-update-slice_fusion.14
  135.5 2.0 constant_dynamic-update-slice_fusion.13
  137.6 1.8 constant_dynamic-update-slice_fusion.12
  139.4 1.8 constant_dynamic-update-slice_fusion.11
  141.2 1.8 constant_dynamic-update-slice_fusion.10
  143.0 1.9 constant_dynamic-update-slice_fusion.9
  144.9 1.8 constant_dynamic-update-slice_fusion.8
  149.9 18.5 %all_gather.21 = f32[2048,8]{0,1:T(8,128)S(1)} all-gather(f32[128,8]{0,1:T(8,128)S(1)} %concatenate.116), channel_id=1, replica_groups=mesh['dp'=32,'seq'=16] {'seq'}, dimensions={0}, use_global_device_ids=true | all-gather | bytes 69632 | tf_op jit(solution)/shard_map/all_gather | solution.py:163
  168.4 16.7 %all_gather.23 = f32[2048,8]{0,1:T(8,128)S(1)} all-gather(f32[128,8]{0,1:T(8,128)S(1)} %concatenate.117), channel_id=1, replica_groups=mesh['dp'=32,'seq'=16] {'seq'}, dimensions={0}, use_global_device_ids=true | all-gather | bytes 69632 | tf_op jit(solution)/shard_map/all_gather | solution.py:164
  189.5 22.6 %all-gather.13.cloned.1.call-done = bf16[1,2048,1024]{2,1,0:T(8,128)(2,1)} async-done(((bf16[1,128,1024]{2,1,0:T(8,128)(2,1)}), bf16[1,2048,1024]{2,1,0:T(8,128)(2,1)}) %all-gather.13.cloned.1.call-update) | async-done | bytes 4194320 | tf_op jit(solution)/shard_map/all_gather | solution.py:169
  237.6 2.4 constant_dynamic-update-slice_fusion.23
  240.1 2.9 constant_dynamic-update-slice_fusion.22
  242.9 2.8 constant_dynamic-update-slice_fusion.21
  245.7 2.8 constant_dynamic-update-slice_fusion.20
  248.5 2.8 constant_dynamic-update-slice_fusion.19
  251.3 2.5 constant_dynamic-update-slice_fusion.18
  253.9 2.5 constant_dynamic-update-slice_fusion.17
  256.4 1.9 constant_dynamic-update-slice_fusion.16
  260.7 98.3 %psum.7 = f32[2,1024]{1,0:T(2,128)S(1)} all-reduce(f32[2,1024]{1,0:T(2,128)S(1)} %pad_maximum_fusion.2), channel_id=1, replica_groups=mesh['dp'=32,'seq'=16] {'dp','seq'}, use_global_device_ids=true, to_apply=%region_26.27 | all-reduce | flops 2048 | bytes 16384 | tf_op jit(solution)/shard_map/psum | solution.py:184
  (161 shorter events, 64.8 us)
Async XLA Ops:
  7.2 62.6 %all-gather.7.cloned.1.call-start = ((), (), s32[]{:S(2)}) async-start(), calls=%async_computation | async-start | bytes 4456448 | tf_op jit(solution)/shard_map/all_gather | solution.py:141
  7.9 63.8 %copy-start.31 = (f32[128]{0:T(128)}, f32[128]{0:T(128)S(1)}, u32[]{:S(2)}) copy-start(f32[128]{0:T(128)S(1)} %convert_bitcast_fusion) | copy-start | bytes 1540
  12.0 59.7 %copy-start.3 = (bf16[128,1024]{0,1:T(8,128)(2,1)S(1)}, bf16[128,1024]{0,1:T(8,128)(2,1)}, u32[]{:S(2)}) copy-start(bf16[128,1024]{0,1:T(8,128)(2,1)} %get-tuple-element.73) | copy-start | bytes 786436
  12.1 101.7 %all-gather.11.cloned.1.call-start = ((), (), s32[]{:S(2)}) async-start(), calls=%async_computation.2 | async-start | bytes 4456448 | tf_op jit(solution)/shard_map/all_gather | solution.py:142
  12.8 174.4 %all-gather.9.cloned.1.call-start = ((), (), s32[]{:S(2)}) async-start(), calls=%async_computation.1 | async-start | bytes 4456448 | tf_op jit(solution)/shard_map/all_gather | solution.py:168
  13.6 198.5 %all-gather.13.cloned.1.call-start = ((), (), s32[]{:S(2)}) async-start(), calls=%async_computation.3 | async-start | bytes 4456448 | tf_op jit(solution)/shard_map/all_gather | solution.py:169
  117.8 4.8 %copy-start = (f32[128,512]{1,0:T(8,128)}, f32[128,512]{1,0:T(8,128)S(1)}, u32[]{:S(2)}) copy-start(f32[128,512]{1,0:T(8,128)S(1)} %get-tuple-element.88) | copy-start | bytes 786436
  118.9 4.6 %copy-start.1 = (f32[128,512]{1,0:T(8,128)}, f32[128,512]{1,0:T(8,128)S(1)}, u32[]{:S(2)}) copy-start(f32[128,512]{1,0:T(8,128)S(1)} %get-tuple-element.90) | copy-start | bytes 786436
  139.4 47.8 %copy-start.11 = (pred[2048,128]{1,0:T(32,128)(4,1)S(1)}, pred[2048,128]{1,0:T(32,128)(4,1)}, u32[]{:S(2)}) copy-start(pred[2048,128]{1,0:T(32,128)(4,1)} %copy.165) | copy-start | bytes 786436
  143.0 70.4 %copy-start.12 = (pred[2048,128]{1,0:T(32,128)(4,1)S(1)}, pred[2048,128]{1,0:T(32,128)(4,1)}, u32[]{:S(2)}) copy-start(pred[2048,128]{1,0:T(32,128)(4,1)} %copy.165) | copy-start | bytes 786436
  223.7 6.9 %copy-start.13 = (pred[2048,128]{1,0:T(32,128)(4,1)S(1)}, pred[2048,128]{1,0:T(32,128)(4,1)}, u32[]{:S(2)}) copy-start(pred[2048,128]{1,0:T(32,128)(4,1)} %copy.165) | copy-start | bytes 786436
  227.2 6.5 %copy-start.26 = (f32[2048,1]{0,1:T(1,128)S(1)}, f32[2048,1]{0,1:T(1,128)}, u32[]{:S(2)}) copy-start(f32[2048,1]{0,1:T(1,128)} %get-tuple-element.59) | copy-start | bytes 24580
  228.9 4.8 %copy-start.4 = (f32[2048,128]{1,0:T(8,128)}, f32[2048,128]{1,0:T(8,128)S(1)}, u32[]{:S(2)}) copy-start(f32[2048,128]{1,0:T(8,128)S(1)} %fusion.17) | copy-start | bytes 3145732
  240.1 11.3 %copy-start.5 = (f32[2048,128]{1,0:T(8,128)S(1)}, f32[2048,128]{1,0:T(8,128)}, u32[]{:S(2)}) copy-start(f32[2048,128]{1,0:T(8,128)} %copy-done.4) | copy-start | bytes 3145732
  251.3 8.6 %copy-start.14 = (f32[128,128]{0,1:T(8,128)S(1)}, f32[128,128]{0,1:T(8,128)}, u32[]{:S(2)}) copy-start(f32[128,128]{0,1:T(8,128)} %get-tuple-element.112) | copy-start | bytes 196612
  253.8 6.1 %copy-start.10 = (f32[128,1024]{0,1:T(8,128)S(1)}, f32[128,1024]{0,1:T(8,128)}, u32[]{:S(2)}) copy-start(f32[128,1024]{0,1:T(8,128)} %constant_dynamic-update-slice_fusion.31) | copy-start | bytes 1572868
  253.8 6.2 %copy-start.15 = (f32[128,128]{0,1:T(8,128)S(1)}, f32[128,128]{0,1:T(8,128)}, u32[]{:S(2)}) copy-start(f32[128,128]{0,1:T(8,128)} %get-tuple-element.114) | copy-start | bytes 196612
  253.8 6.2 %copy-start.16 = (f32[128,128]{0,1:T(8,128)S(1)}, f32[128,128]{0,1:T(8,128)}, u32[]{:S(2)}) copy-start(f32[128,128]{0,1:T(8,128)} %get-tuple-element.116) | copy-start | bytes 196612
  253.8 6.2 %copy-start.17 = (f32[128,128]{0,1:T(8,128)S(1)}, f32[128,128]{0,1:T(8,128)}, u32[]{:S(2)}) copy-start(f32[128,128]{0,1:T(8,128)} %get-tuple-element.118) | copy-start | bytes 196612
  253.8 6.2 %copy-start.18 = (f32[128,128]{0,1:T(8,128)S(1)}, f32[128,128]{0,1:T(8,128)}, u32[]{:S(2)}) copy-start(f32[128,128]{0,1:T(8,128)} %get-tuple-element.120) | copy-start | bytes 196612
  253.8 6.3 %copy-start.19 = (f32[128,128]{0,1:T(8,128)S(1)}, f32[128,128]{0,1:T(8,128)}, u32[]{:S(2)}) copy-start(f32[128,128]{0,1:T(8,128)} %get-tuple-element.122) | copy-start | bytes 196612
  253.8 6.3 %copy-start.20 = (f32[128,128]{0,1:T(8,128)S(1)}, f32[128,128]{0,1:T(8,128)}, u32[]{:S(2)}) copy-start(f32[128,128]{0,1:T(8,128)} %get-tuple-element.126) | copy-start | bytes 196612
  253.9 6.3 %copy-start.21 = (f32[128,128]{0,1:T(8,128)S(1)}, f32[128,128]{0,1:T(8,128)}, u32[]{:S(2)}) copy-start(f32[128,128]{0,1:T(8,128)} %get-tuple-element.128) | copy-start | bytes 196612
  253.9 6.3 %copy-start.22 = (f32[128,128]{0,1:T(8,128)S(1)}, f32[128,128]{0,1:T(8,128)}, u32[]{:S(2)}) copy-start(f32[128,128]{0,1:T(8,128)} %get-tuple-element.130) | copy-start | bytes 196612
  (13 other events, 37.2 us)
Sparse Core Ops, SparseCore 0:
  12.2 57.5 all-gather.6
  71.9 41.7 all-gather.10
  116.4 51.6 all-gather.8
  170.1 41.9 all-gather.12
where the time goes:
time: 368 us; the launch traced here: 366 us
  blocking collectives  133 us (36%)
  waiting for transfers between devices  116 us (32%)
  matrix products  74.5 us (20%)
  local copies, waits for them, and re-layouts  20.3 us (6%)
  between operations  14.5 us (4%)
  other arithmetic  7.21 us (2%)
    psum x1, blocking collectives, body(): cond_grad = lax.psum(jnp.stack([partial_value, key_partial]), ('dp', 'seq'))  98.3 us
    all_gather x1, waiting for transfers between devices, body(): lax.all_gather(key_eff, 'seq', axis=0, tiled=True)  50.2 us
    all_gather x1, waiting for transfers between devices, body(): lax.all_gather(value_rows, 'seq', axis=0, tiled=True)  41.4 us
    dot_general x16, matrix products, contract_first(): lax.dot_general(left, right, (((0,), (0,)), ((), ())), preferred_element_...  33.7 us
    all_gather x1, waiting for transfers between devices, body(): grad_piece = lax.all_gather(grad_rows, 'seq', axis=0, tiled=True)  22.6 us
    all_gather x1, blocking collectives, body(): lax.all_gather(log_totals, 'seq', axis=0, tiled=True)  18.5 us
    dot_general x16, matrix products, contract_last(): lax.dot_general(left, right, (((1,), (1,)), ((), ())), preferred_element_...  18.5 us
    all_gather x1, blocking collectives, body(): lax.all_gather(deltas, 'seq', axis=0, tiled=True)  16.7 us
  transfers between devices with their start and end apart: 4, of which 3 were waited for; matrix products, arithmetic and copies ran while one was open for 13% of the time, Pallas kernels for 0%

commit v1 on v0

--- a/solution.py
+++ b/solution.py
@@ -181,7 +181,9 @@
     key_total = grads[0]
     value_total = grads[1]
     key_partial = jnp.sum(flag_column * key_total, axis=0)
-    cond_grad = lax.psum(jnp.stack([partial_value, key_partial]), ("dp", "seq"))
+    own = jnp.stack([partial_value, key_partial])
+    parts = lax.all_gather(own, ("dp", "seq"))
+    cond_grad = jnp.sum(parts, axis=0)
     cond_grad = cond_grad / graph_count
     return (
         attended[None],

time: 368 us -> 1090 us (2.96)
  waiting for transfers between devices: 116 us -> 932 us
  blocking collectives: 133 us -> 36.8 us
    all_gather x0 -> x1, waiting for transfers between devices: none -> 806 us  [body(): parts = lax.all_gather(own, ('dp', 'seq'))]
    psum x1 -> x0, blocking collectives: 98.3 us -> none  [body(): cond_grad = lax.psum(jnp.stack([partial_value, key_partial]), ('dp', 'seq'))]
    all_gather x1, waiting for transfers between devices: 22.6 us -> 35.4 us  [body(): grad_piece = lax.all_gather(grad_rows, 'seq', axis=0, tiled=True)]
  transfers between devices with their start and end apart: 4 -> 5, of which waited for: 3 -> 4; matrix products, arithmetic and copies ran while one was open for 13% -> 4% of each run, Pallas kernels for 0% -> 0%
where the time goes in v1:
time: 1090 us
  waiting for transfers between devices  932 us (86%)
  matrix products  67.9 us (6%)
  blocking collectives  36.8 us (3%)
  local copies, waits for them, and re-layouts  25.4 us (2%)
  between operations  14.5 us (1%)
    all_gather x1, waiting for transfers between devices, body(): parts = lax.all_gather(own, ('dp', 'seq'))  806 us
    all_gather x1, waiting for transfers between devices, body(): lax.all_gather(key_eff, 'seq', axis=0, tiled=True)  50.1 us
    all_gather x1, waiting for transfers between devices, body(): lax.all_gather(value_rows, 'seq', axis=0, tiled=True)  38.7 us
    all_gather x1, waiting for transfers between devices, body(): grad_piece = lax.all_gather(grad_rows, 'seq', axis=0, tiled=True)  35.4 us
    dot_general x16, matrix products, contract_first(): lax.dot_general(left, right, (((0,), (0,)), ((), ())), preferred_element_...  29.2 us
  transfers between devices with their start and end apart: 5, of which 4 were waited for; matrix products, arithmetic and copies ran while one was open for 4% of the time, Pallas kernels for 0%

profile of v1, /device:TPU:1, one launch (start us, length us, event | category | flops | bytes accessed | tf_op | source)
XLA Modules:
  0.0 1087.4 jit_solution(18270756025777154360)
XLA Ops:
  19.7 50.1 %all-gather.10.cloned.1.call-done = bf16[2048,1024]{0,1:T(8,128)(2,1)} async-done(((bf16[128,1024]{0,1:T(8,128)(2,1)}), bf16[2048,1024]{0,1:T(8,128)(2,1)}) %all-gather.10.cloned.1.call-update) | async-done | bytes 4194320 | tf_op jit(solution)/shard_map/all_gather | solution.py:141
  75.1 38.7 %all-gather.14.cloned.1.call-done = bf16[1,2048,1024]{2,1,0:T(8,128)(2,1)} async-done(((bf16[1,128,1024]{2,1,0:T(8,128)(2,1)}), bf16[1,2048,1024]{2,1,0:T(8,128)(2,1)}) %all-gather.14.cloned.1.call-update) | async-done | bytes 4194320 | tf_op jit(solution)/shard_map/all_gather | solution.py:142
  119.0 20.0 %all_gather.27 = f32[2048,8]{0,1:T(8,128)} all-gather(f32[128,8]{0,1:T(8,128)S(1)} %concatenate.116), channel_id=1, replica_groups=mesh['dp'=32,'seq'=16] {'seq'}, dimensions={0}, use_global_device_ids=true | all-gather | bytes 69632 | tf_op jit(solution)/shard_map/all_gather | solution.py:163
  139.0 16.8 %all_gather.29 = f32[2048,8]{0,1:T(8,128)S(1)} all-gather(f32[128,8]{0,1:T(8,128)S(1)} %concatenate.117), channel_id=1, replica_groups=mesh['dp'=32,'seq'=16] {'seq'}, dimensions={0}, use_global_device_ids=true | all-gather | bytes 69632 | tf_op jit(solution)/shard_map/all_gather | solution.py:164
  155.8 2.0 constant_dynamic-update-slice_fusion.15
  159.3 2.0 constant_dynamic-update-slice_fusion.14
  161.3 2.0 constant_dynamic-update-slice_fusion.13
  176.7 35.4 %all-gather.16.cloned.1.call-done = bf16[1,2048,1024]{2,1,0:T(8,128)(2,1)} async-done(((bf16[1,128,1024]{2,1,0:T(8,128)(2,1)}), bf16[1,2048,1024]{2,1,0:T(8,128)(2,1)}) %all-gather.16.cloned.1.call-update) | async-done | bytes 4194320 | tf_op jit(solution)/shard_map/all_gather | solution.py:169
  212.1 2.4 constant_dynamic-update-slice_fusion.23
  217.7 2.4 constant_dynamic-update-slice_fusion.22
  222.5 2.4 constant_dynamic-update-slice_fusion.21
  225.6 2.8 fusion.29
  228.4 2.8 constant_dynamic-update-slice_fusion.20
  231.8 2.8 fusion.23
  234.5 2.8 constant_dynamic-update-slice_fusion.19
  237.9 2.7 fusion.17
  240.7 2.8 constant_dynamic-update-slice_fusion.18
  244.1 2.7 fusion.11
  246.8 2.8 constant_dynamic-update-slice_fusion.17
  250.2 2.7 fusion.5
  253.0 2.8 constant_dynamic-update-slice_fusion.16
  262.8 1.9 fusion.115
  271.1 805.8 %all-gather.18.cloned.1.call-done = f32[512,2,1024]{2,1,0:T(2,128)} async-done(((f32[1,2,1024]{2,1,0:T(2,128)}), f32[512,2,1024]{2,1,0:T(2,128)}) %all-gather.18.cloned.1.call-update) | async-done | bytes 4194320 | tf_op jit(solution)/shard_map/all_gather | solution.py:185
  1076.9 3.4 reduce_sum.189
  (200 shorter events, 60.0 us)
Async XLA Ops:
  7.2 62.6 %all-gather.10.cloned.1.call-start = ((), (), s32[]{:S(2)}) async-start(), calls=%async_computation | async-start | bytes 4456448 | tf_op jit(solution)/shard_map/all_gather | solution.py:141
  7.9 63.7 %copy-start.40 = (f32[128]{0:T(128)}, f32[128]{0:T(128)S(1)}, u32[]{:S(2)}) copy-start(f32[128]{0:T(128)S(1)} %convert_bitcast_fusion) | copy-start | bytes 1540
  12.0 59.7 %copy-start.7 = (bf16[128,1024]{0,1:T(8,128)(2,1)S(1)}, bf16[128,1024]{0,1:T(8,128)(2,1)}, u32[]{:S(2)}) copy-start(bf16[128,1024]{0,1:T(8,128)(2,1)} %get-tuple-element.78) | copy-start | bytes 786436
  12.1 101.7 %all-gather.14.cloned.1.call-start = ((), (), s32[]{:S(2)}) async-start(), calls=%async_computation.2 | async-start | bytes 4456448 | tf_op jit(solution)/shard_map/all_gather | solution.py:142
  12.8 161.5 %all-gather.12.cloned.1.call-start = ((), (), s32[]{:S(2)}) async-start(), calls=%async_computation.1 | async-start | bytes 4456448 | tf_op jit(solution)/shard_map/all_gather | solution.py:168
  13.6 198.6 %all-gather.16.cloned.1.call-start = ((), (), s32[]{:S(2)}) async-start(), calls=%async_computation.3 | async-start | bytes 4456448 | tf_op jit(solution)/shard_map/all_gather | solution.py:169
  14.1 1062.7 %all-gather.18.cloned.1.call-start = ((), (), s32[]{:S(2)}) async-start(), calls=%async_computation.4 | async-start | bytes 4202496 | tf_op jit(solution)/shard_map/all_gather | solution.py:185
  75.0 42.7 %copy-start.35 = (f32[128]{0:T(128)}, f32[128]{0:T(128)S(1)}, u32[]{:S(2)}) copy-start(f32[128]{0:T(128)S(1)} %get-tuple-element.147) | copy-start | bytes 1540
  75.0 42.6 %copy-start.36 = (f32[128]{0:T(128)}, f32[128]{0:T(128)S(1)}, u32[]{:S(2)}) copy-start(f32[128]{0:T(128)S(1)} %get-tuple-element.148) | copy-start | bytes 1540
  75.0 42.6 %copy-start.37 = (f32[128]{0:T(128)}, f32[128]{0:T(128)S(1)}, u32[]{:S(2)}) copy-start(f32[128]{0:T(128)S(1)} %get-tuple-element.149) | copy-start | bytes 1540
  75.0 42.6 %copy-start.38 = (f32[128]{0:T(128)}, f32[128]{0:T(128)S(1)}, u32[]{:S(2)}) copy-start(f32[128]{0:T(128)S(1)} %get-tuple-element.150) | copy-start | bytes 1540
  75.1 42.6 %copy-start.39 = (f32[128]{0:T(128)}, f32[128]{0:T(128)S(1)}, u32[]{:S(2)}) copy-start(f32[128]{0:T(128)S(1)} %get-tuple-element.151) | copy-start | bytes 1540
  155.8 14.8 %copy-start.43 = (f32[128]{0:T(128)S(1)}, f32[128]{0:T(128)}, u32[]{:S(2)}) copy-start(f32[128]{0:T(128)} %copy-done.42) | copy-start | bytes 1540
  166.9 48.2 %copy-start.14 = (f32[128,1024]{0,1:T(8,128)S(1)}, f32[128,1024]{0,1:T(8,128)}, u32[]{:S(2)}) copy-start(f32[128,1024]{0,1:T(8,128)} %constant_dynamic-update-slice_fusion.31) | copy-start | bytes 1572868
  168.8 46.4 %copy-start.20 = (f32[128,128]{0,1:T(8,128)S(1)}, f32[128,128]{0,1:T(8,128)}, u32[]{:S(2)}) copy-start(f32[128,128]{0,1:T(8,128)} %get-tuple-element.115) | copy-start | bytes 196612
  168.8 46.4 %copy-start.21 = (f32[128,128]{0,1:T(8,128)S(1)}, f32[128,128]{0,1:T(8,128)}, u32[]{:S(2)}) copy-start(f32[128,128]{0,1:T(8,128)} %get-tuple-element.117) | copy-start | bytes 196612
  168.8 46.4 %copy-start.22 = (f32[128,128]{0,1:T(8,128)S(1)}, f32[128,128]{0,1:T(8,128)}, u32[]{:S(2)}) copy-start(f32[128,128]{0,1:T(8,128)} %get-tuple-element.119) | copy-start | bytes 196612
  168.8 46.4 %copy-start.23 = (f32[128,128]{0,1:T(8,128)S(1)}, f32[128,128]{0,1:T(8,128)}, u32[]{:S(2)}) copy-start(f32[128,128]{0,1:T(8,128)} %get-tuple-element.121) | copy-start | bytes 196612
  170.6 44.6 %copy-start.24 = (f32[128,128]{0,1:T(8,128)S(1)}, f32[128,128]{0,1:T(8,128)}, u32[]{:S(2)}) copy-start(f32[128,128]{0,1:T(8,128)} %get-tuple-element.123) | copy-start | bytes 196612
  170.6 44.6 %copy-start.25 = (f32[128,128]{0,1:T(8,128)S(1)}, f32[128,128]{0,1:T(8,128)}, u32[]{:S(2)}) copy-start(f32[128,128]{0,1:T(8,128)} %get-tuple-element.125) | copy-start | bytes 196612
  172.4 43.7 %copy-start.17 = (pred[2048,128]{1,0:T(32,128)(4,1)S(1)}, pred[2048,128]{1,0:T(32,128)(4,1)}, u32[]{:S(2)}) copy-start(pred[2048,128]{1,0:T(32,128)(4,1)} %copy.222) | copy-start | bytes 786436
  176.1 44.7 %copy-start.13 = (bf16[128,1024]{0,1:T(8,128)(2,1)S(1)}, bf16[128,1024]{0,1:T(8,128)(2,1)}, u32[]{:S(2)}) copy-start(bf16[128,1024]{0,1:T(8,128)(2,1)} %get-tuple-element.79) | copy-start | bytes 786436
  224.9 9.6 copy-start.32
  246.8 9.6 copy-start.41
  (32 other events, 129.8 us)
Sparse Core Ops, SparseCore 0:
  12.2 57.5 all-gather.9
  71.9 41.8 all-gather.13
  116.4 52.3 all-gather.11
  170.8 41.2 all-gather.15
  258.7 818.1 all-gather.17
